TPU v7x, 128 devices: a whole 4x4x4 slice. The times are simulated.
128 devices in a mesh: seq: 32 (over z, x, y_lo), tp: 4 (over y_hi, core).
Axes of the slice: x: 4, y: 4 (y_hi: 2, y_lo: 2; y = y_hi * 2 + y_lo), z: 4, core: 2. Of those that a mesh axis runs over, the one named last changes fastest.
Arguments:
- query_gate: bfloat16 [256, 131072], P('tp', 'seq'), may hold values from -6 to 6
- key_gate: bfloat16 [256, 131072], P('tp', 'seq'), may hold values from -6 to 6
- value_input: bfloat16 [256, 131072], P('tp', 'seq'), may hold values from -6 to 6
- long_filter: float32 [256, 131072], P('tp', 'seq'), may hold values from -2 to 2, as said below
- out_weight: bfloat16 [256, 256], replicated, may hold values from -0.375 to 0.375
Outputs:
- mixed: bfloat16 [256, 131072], P('tp', 'seq')
Inputs may be any that keep to these rules, and one draw needn't show every extreme that they name: `long_filter`: each channel's taps follow a decaying envelope.
All inputs are finite; a program needn't handle non-finite values.
Results may differ from a plain program's by a relative error of at most 0.018.
Values may be sent and summed in bfloat16 or wider, within the bound.
No kernel may reach another device: no remote copies, remote signals or barrier semaphores. Data moves between devices by JAX's collectives and lax.ppermute only.
A program may use at most 64 MiB of HBM per device.

v0:
```python
import math

import jax
import jax.numpy as jnp
from jax import lax
from jax.sharding import PartitionSpec as P

HIGH = lax.Precision.HIGH


def angle_table(row_count, col_count, modulus, row_start, col_start):
    row_ids = lax.broadcasted_iota(jnp.int32, (row_count, col_count), 0) + row_start
    col_ids = lax.broadcasted_iota(jnp.int32, (row_count, col_count), 1) + col_start
    return angles_of(row_ids * col_ids, modulus)


def angles_of(products, modulus):
    angles = (products % modulus).astype(jnp.float32) * (2.0 * math.pi / modulus)
    return (jnp.cos(angles), jnp.sin(angles))


def slot_rows(device, slot, seqs):
    return jnp.where(slot == 0, device, jnp.where(device == 0, seqs, 2 * seqs - device))


def major(table, data):
    return jnp.einsum("qk,k...->q...", table, data, precision=HIGH)


def minor(data, table):
    return jnp.einsum("...b,bm->...m", data, table, precision=HIGH)


def negated_grid(flipped):
    tail = jnp.roll(flipped[-1:], 1, axis=flipped.ndim - 1)
    return jnp.concatenate([tail, flipped[:-1]], axis=0)


def body(query_gate, key_gate, value_input, long_filter, out_weight):
    chans, length = key_gate.shape
    seqs = lax.axis_size("seq")
    seq_index = lax.axis_index("seq")
    width = length // seqs
    rows = 2 * seqs
    full = rows * length
    pairs = chans // 2
    f32, bf16 = jnp.float32, jnp.bfloat16

    gated = (key_gate.astype(f32) * value_input.astype(f32)).astype(bf16)
    taps = long_filter.astype(bf16)
    both = jnp.concatenate([gated[:pairs], taps[:pairs], gated[pairs:], taps[pairs:]], axis=0)
    send = both.reshape(2 * chans, seqs, width).transpose(1, 0, 2)
    got = lax.all_to_all(send, "seq", 0, 0, tiled=True).astype(f32)
    packed_real, packed_imag = got[:, :chans], got[:, chans:]

    slot_dev = lax.broadcasted_iota(jnp.int32, (seqs, 2), 0).reshape(rows, 1)
    slot_idx = lax.broadcasted_iota(jnp.int32, (seqs, 2), 1).reshape(rows, 1)
    row_of_slot = slot_rows(slot_dev, slot_idx, seqs)
    cos_a, sin_a = angles_of(row_of_slot * lax.broadcasted_iota(jnp.int32, (rows, seqs), 1), rows)
    freq_real = major(cos_a, packed_real) + major(sin_a, packed_imag)
    freq_imag = major(cos_a, packed_imag) - major(sin_a, packed_real)
    cols = lax.broadcasted_iota(jnp.int32, (rows, width), 1) + seq_index * width
    cos_t, sin_t = angles_of(row_of_slot * cols, full)
    cos_t, sin_t = cos_t[:, None, :], sin_t[:, None, :]
    spread_real = freq_real * cos_t + freq_imag * sin_t
    spread_imag = freq_imag * cos_t - freq_real * sin_t
    spread = jnp.stack([spread_real, spread_imag], axis=1).astype(bf16)
    spread = spread.reshape(seqs, 2, 2, chans, width)
    recv = lax.all_to_all(spread, "seq", 0, 0, tiled=True).astype(f32)
    rows_real, rows_imag = recv[:, :, 0], recv[:, :, 1]

    cos_o, sin_o = angle_table(seqs, seqs, seqs, 0, 0)
    cos_w, sin_w = angle_table(seqs, width, length, 0, 0)
    cos_w, sin_w = cos_w[:, None, None, :], sin_w[:, None, None, :]
    cos_i, sin_i = angle_table(width, width, width, 0, 0)
    first_real = major(cos_o, rows_real) + major(sin_o, rows_imag)
    first_imag = major(cos_o, rows_imag) - major(sin_o, rows_real)
    twist_real = first_real * cos_w + first_imag * sin_w
    twist_imag = first_imag * cos_w - first_real * sin_w
    spec_real = minor(twist_real, cos_i) + minor(twist_imag, sin_i)
    spec_imag = minor(twist_imag, cos_i) - minor(twist_real, sin_i)

    def self_paired(parts):
        flipped = [jnp.flip(part, axis=(0, 3)) for part in parts]
        return tuple(jnp.stack([negated_grid(f[:, 0]), f[:, 1]], axis=1) for f in flipped)

    def cross_paired(parts):
        return tuple(jnp.flip(part, axis=(0, 1, 3)) for part in parts)

    neg_real, neg_imag = lax.cond(
        seq_index == 0, self_paired, cross_paired, (spec_real, spec_imag)
    )

    a_real = 0.5 * (spec_real + neg_real)
    a_imag = 0.5 * (spec_imag - neg_imag)
    b_real = 0.5 * (spec_imag + neg_imag)
    b_imag = 0.5 * (neg_real - spec_real)
    sig1_r, sig1_i, filt1_r, filt1_i = (
        a_real[:, :, :pairs], a_imag[:, :, :pairs], a_real[:, :, pairs:], a_imag[:, :, pairs:]
    )
    sig2_r, sig2_i, filt2_r, filt2_i = (
        b_real[:, :, :pairs], b_imag[:, :, :pairs], b_real[:, :, pairs:], b_imag[:, :, pairs:]
    )
    prod1_r = sig1_r * filt1_r - sig1_i * filt1_i
    prod1_i = sig1_r * filt1_i + sig1_i * filt1_r
    prod2_r = sig2_r * filt2_r - sig2_i * filt2_i
    prod2_i = sig2_r * filt2_i + sig2_i * filt2_r
    prod_real = prod1_r - prod2_i
    prod_imag = prod1_i + prod2_r

    inv_real = minor(prod_real, cos_i) - minor(prod_imag, sin_i)
    inv_imag = minor(prod_imag, cos_i) + minor(prod_real, sin_i)
    untwist_real = inv_real * cos_w - inv_imag * sin_w
    untwist_imag = inv_imag * cos_w + inv_real * sin_w
    back_real = major(cos_o, untwist_real) - major(sin_o, untwist_imag)
    back_imag = major(cos_o, untwist_imag) + major(sin_o, untwist_real)

    own_rows = slot_rows(seq_index, lax.broadcasted_iota(jnp.int32, (2, length), 0), seqs)
    cos_b, sin_b = angles_of(own_rows * lax.broadcasted_iota(jnp.int32, (2, length), 1), full)
    cos_b = cos_b.reshape(2, seqs, width).transpose(1, 0, 2)[:, :, None, :]
    sin_b = sin_b.reshape(2, seqs, width).transpose(1, 0, 2)[:, :, None, :]
    reverted_real = back_real * cos_b - back_imag * sin_b
    reverted_imag = back_imag * cos_b + back_real * sin_b
    reverted = jnp.stack([reverted_real, reverted_imag], axis=2).astype(bf16)
    moved = lax.all_to_all(reverted, "seq", 0, 0, tiled=True).astype(f32)
    moved = moved.reshape(rows, 2, pairs, width)

    blocks = lax.broadcasted_iota(jnp.int32, (seqs, rows), 0)
    cos_l, sin_l = angles_of(blocks * row_of_slot.reshape(1, rows), rows)
    merged_real = major(cos_l, moved[:, 0]) - major(sin_l, moved[:, 1])
    merged_imag = major(cos_l, moved[:, 1]) + major(sin_l, moved[:, 0])
    merged = jnp.concatenate([merged_real, merged_imag], axis=1) * (1.0 / full)
    arrived = lax.all_to_all(merged.astype(bf16), "seq", 0, 0, tiled=True)
    conv = arrived.astype(f32).transpose(1, 0, 2).reshape(chans, length)
    gated_out = (query_gate.astype(f32) * conv).astype(bf16)

    tp_index = lax.axis_index("tp")
    core = tp_index % 2
    half = tp_index // 2
    tps = lax.axis_size("tp")
    columns = lax.dynamic_slice_in_dim(out_weight, tp_index * chans, chans, 1)
    grouped = columns.reshape(2, 2, chans, chans)
    keep_w = lax.dynamic_index_in_dim(grouped, core, 1, keepdims=False)
    send_w = lax.dynamic_index_in_dim(grouped, 1 - core, 1, keepdims=False)
    send_part = jnp.einsum("hoc,cp->hop", send_w, gated_out, preferred_element_type=f32)
    keep_part = jnp.einsum("hoc,cp->hop", keep_w, gated_out, preferred_element_type=f32)
    pair = [(i, i ^ 1) for i in range(tps)]
    chip_sum = keep_part + lax.ppermute(send_part.astype(bf16), "tp", pair).astype(f32)
    keep_chip = lax.dynamic_index_in_dim(chip_sum, half, 0, keepdims=False)
    send_chip = lax.dynamic_index_in_dim(chip_sum, 1 - half, 0, keepdims=False)
    cross = [(i, i ^ 2) for i in range(tps)]
    total = keep_chip + lax.ppermute(send_chip.astype(bf16), "tp", cross).astype(f32)
    return total.astype(bf16)


def solution(mesh):
    return jax.shard_map(
        body,
        mesh=mesh,
        in_specs=(P("tp", "seq"), P("tp", "seq"), P("tp", "seq"), P("tp", "seq"), P()),
        out_specs=P("tp", "seq"),
        check_vma=False,
    )
```

profile of v0, /device:TPU:1, one launch (start us, length us, event | category | flops | bytes accessed | tf_op | source)
XLA Modules:
  0.0 192.0 jit_solution(16890574925884597917)
XLA Ops:
  0.0 1.3 convert_element_type.149
  1.3 1.3 multiply_convert_fusion
  2.8 0.7 copy.93
  3.5 1.3 copy.94
  4.8 9.7 %all-to-all-start = ((bf16[32,128,128]{2,1,0:T(8,128)(2,1)}), bf16[32,128,128]{2,1,0:T(8,128)(2,1)S(1)}, u32[]{:S(2)}, u32[]{:S(2)}) async-start(bf16[32,128,128]{2,1,0:T(8,128)(2,1)} %copy.94), calls=%async_computation | async-start | bytes 2097152 | tf_op jit(solution)/shard_map/all_to_all | solution.py:53
  15.0 16.2 %all-to-all-done = bf16[32,128,128]{2,1,0:T(8,128)(2,1)S(1)} async-done(((bf16[32,128,128]{2,1,0:T(8,128)(2,1)}), bf16[32,128,128]{2,1,0:T(8,128)(2,1)S(1)}, u32[]{:S(2)}, u32[]{:S(2)}) %all-to-all-start) | async-done | bytes 1048608 | tf_op jit(solution)/shard_map/all_to_all | solution.py:53
  31.3 0.9 fusion.35
  32.2 0.9 fusion.31
  33.0 1.0 convolution_add_fusion.1
  34.1 1.5 add_convert_fusion
  35.6 1.2 copy.97
  36.8 1.2 copy.98
  38.0 1.5 pad_maximum_fusion.2
  39.5 4.3 %all-to-all-start.1 = ((bf16[32,2,2,64,128]{4,3,1,2,0:T(8,128)(2,1)}), bf16[32,2,2,64,128]{4,3,1,2,0:T(8,128)(2,1)S(1)}, u32[]{:S(2)}, u32[]{:S(2)}) async-start(bf16[32,2,2,64,128]{4,3,1,2,0:T(8,128)(2,1)} %pad_maximum_fusion.2), calls=%async_computation.1 | async-start | bytes 4194304 | tf_op jit(solution)/shard_map/all_to_all | solution.py:69
  44.1 27.1 %all-to-all-done.1 = bf16[32,2,2,64,128]{4,3,1,2,0:T(8,128)(2,1)S(1)} async-done(((bf16[32,2,2,64,128]{4,3,1,2,0:T(8,128)(2,1)}), bf16[32,2,2,64,128]{4,3,1,2,0:T(8,128)(2,1)S(1)}, u32[]{:S(2)}, u32[]{:S(2)}) %all-to-all-start.1) | async-done | bytes 2097184 | tf_op jit(solution)/shard_map/all_to_all | solution.py:69
  71.4 1.1 fusion.23
  72.5 1.1 fusion.24
  73.7 1.1 convolution_add_fusion
  74.8 1.6 multiply_add_fusion
  76.5 2.3 %fusion.2 = f32[32,2,64,128]{3,2,1,0:T(8,128)S(1)} fusion(f32[32,2,64,128]{3,0,2,1:T(8,128)S(1)} %get-tuple-element.28), kind=kOutput, calls=%fused_computation.17 | convolution fusion | flops 402882560 | bytes 4194304 | tf_op jit(solution)/shard_map/...b,bm->...m/dot_general | solution.py:31
  78.7 2.2 %fusion = f32[32,2,64,128]{3,2,1,0:T(8,128)S(1)} fusion(f32[32,2,64,128]{3,0,2,1:T(8,128)S(1)} %get-tuple-element.28), kind=kOutput, calls=%fused_computation.15 | convolution fusion | flops 402882560 | bytes 4194304 | tf_op jit(solution)/shard_map/...b,bm->...m/dot_general | solution.py:31
  81.0 15.0 %fusion.8 = f32[32,2,64,128]{3,2,1,0:T(8,128)} fusion(f32[32,2,64,128]{3,2,1,0:T(8,128)S(1)} %fusion.2, f32[32,2,64,128]{3,0,2,1:T(8,128)S(1)} %get-tuple-element.27), kind=kOutput, calls=%fused_computation.25 | convolution fusion | flops 403406848 | bytes 6291456 | tf_op jit(solution)/shard_map/...b,bm->...m/dot_general | solution.py:31
  96.0 2.3 %fusion.11 = f32[32,2,64,128]{3,2,1,0:T(8,128)S(1)} fusion(f32[32,2,64,128]{3,2,1,0:T(8,128)S(1)} %fusion, f32[32,2,64,128]{3,0,2,1:T(8,128)S(1)} %get-tuple-element.27), kind=kOutput, calls=%fused_computation.26 | convolution fusion | flops 403406848 | bytes 6291456 | tf_op jit(solution)/shard_map/...b,bm->...m/dot_general | solution.py:31
  98.3 19.9 %conditional.1 = ((f32[32,2,64,128]{3,2,1,0:T(8,128)}, f32[32,2,64,128]{3,2,1,0:T(8,128)})) conditional(s32[]{:T(128)} %convert_element_type.153, (f32[32,2,64,128]{3,2,1,0:T(8,128)}, f32[32,2,64,128]{3,2,1,0:T(8,128)S(1)}) %tuple.13, (f32[32,2,64,128]{3,2,1,0:T(8,128)}, f32[32,2,64,128]{3,2,1,0:T(8,128)S(1)}) %tuple.13), branch_computations={%region_0.1_spmd, %region_1.2_spmd} | conditional | flops 2097152 | bytes 37749768 | solution.py:90
  98.3 0.8 slice.88
  99.3 1.7 copy.89
  101.0 1.0 slice.146
  102.0 1.8 slice.94
  103.9 1.1 maximum_bitcast_fusion
  105.1 0.2 copy.90
  105.3 1.1 slice.149
  106.4 1.8 slice.104
  108.2 1.1 maximum_bitcast_fusion.1
  109.4 1.4 slice.107
  110.8 1.3 slice.96
  112.1 1.4 slice.97
  113.5 4.8 %pad_maximum_fusion = (f32[32,2,64,128]{3,2,1,0:T(8,128)}, f32[32,2,64,128]{3,2,1,0:T(8,128)}) fusion(f32[32,1,64,128]{3,2,1,0:T(8,128)} %slice.97, f32[32,1,64,128]{3,2,1,0:T(8,128)} %maximum_bitcast_fusion, f32[32,1,64,128]{3,2,1,0:T(8,128)} %slice.107, f32[32,1,64,128]{3,2,1,0:T(8,128)} %maximum_bitcast_fusion.1), kind=kLoop, calls=%fused_computation | loop fusion | flops 1048576 | bytes 8388608 | tf_op jit(solution)/shard_map/cond/branch_1_fun/stack | solution.py:85
  118.2 2.9 %add_multiply_fusion.1 = (f32[32,2,64,128]{3,2,1,0:T(8,128)S(1)}, f32[32,2,64,128]{3,2,1,0:T(8,128)S(1)}) fusion(f32[32,2,64,128]{3,2,1,0:T(8,128)} %fusion.8, f32[32,2,64,128]{3,2,1,0:T(8,128)} %get-tuple-element.19), kind=kLoop, calls=%fused_computation.10 | loop fusion | flops 2097152 | bytes 8388608 | tf_op jit(solution)/shard_map/mul | solution.py:94
  121.1 0.5 subtract_multiply_fusion.1
  121.6 1.0 add_subtract_fusion
  122.7 0.8 fusion.44
  123.5 0.8 fusion.46
  124.3 0.8 convolution_add_fusion.3
  125.2 0.9 multiply_add_fusion.1
  126.1 1.2 fusion.17
  127.3 1.2 fusion.21
  128.5 1.2 convolution_add_fusion.2
  129.7 1.5 fusion.25
  131.3 0.4 copy.109
  131.7 17.7 %all_to_all.20 = bf16[32,2,2,32,128]{4,3,1,2,0:T(8,128)(2,1)S(1)} all-to-all(bf16[32,2,2,32,128]{4,3,1,2,0:T(8,128)(2,1)S(1)} %copy.109), channel_id=1, replica_groups=mesh['seq'=32,'tp'=4] {'seq'}, dimensions={0} | all-to-all | bytes 2097152 | tf_op jit(solution)/shard_map/all_to_all | solution.py:125
  149.6 0.4 fusion.29
  150.0 0.4 fusion.30
  150.4 0.5 convolution_subtract_fusion.4
  150.9 0.5 convolution_add_fusion.4
  151.5 1.0 copy.113
  152.5 4.0 %all-to-all-start.3 = ((bf16[32,64,128]{2,1,0:T(8,128)(2,1)}), bf16[32,64,128]{2,1,0:T(8,128)(2,1)S(1)}, u32[]{:S(2)}, u32[]{:S(2)}) async-start(bf16[32,64,128]{2,1,0:T(8,128)(2,1)} %copy.113), calls=%async_computation.3 | async-start | bytes 1048576 | tf_op jit(solution)/shard_map/all_to_all | solution.py:133
  156.6 9.7 %all-to-all-done.3 = bf16[32,64,128]{2,1,0:T(8,128)(2,1)S(1)} async-done(((bf16[32,64,128]{2,1,0:T(8,128)(2,1)}), bf16[32,64,128]{2,1,0:T(8,128)(2,1)S(1)}, u32[]{:S(2)}, u32[]{:S(2)}) %all-to-all-start.3) | async-done | bytes 524320 | tf_op jit(solution)/shard_map/all_to_all | solution.py:133
  166.4 0.4 convolution_convert_fusion
  166.8 5.2 %collective-permute-start = (bf16[2,64,4096]{2,1,0:T(8,128)(2,1)S(1)}, bf16[2,64,4096]{2,1,0:T(8,128)(2,1)}, u32[]{:S(2)}, u32[]{:S(2)}) collective-permute-start(bf16[2,64,4096]{2,1,0:T(8,128)(2,1)S(1)} %convolution_convert_fusion), channel_id=1, source_target_pairs={{0,1},{1,0},{2,3},{3,2},{4,5},{5,4},{6,7},{7,6},{8,9},{9,8},{10,11... | collective-permute-start | bytes 3145736 | tf_op jit(solution)/shard_map/ppermute | solution.py:148
  172.0 2.4 %collective-permute-done = bf16[2,64,4096]{2,1,0:T(8,128)(2,1)} collective-permute-done((bf16[2,64,4096]{2,1,0:T(8,128)(2,1)S(1)}, bf16[2,64,4096]{2,1,0:T(8,128)(2,1)}, u32[]{:S(2)}, u32[]{:S(2)}) %collective-permute-start) | collective-permute-done | bytes 1048608 | tf_op jit(solution)/shard_map/ppermute | solution.py:148
  174.5 1.6 convert_add_fusion
  176.2 2.7 %collective-permute-start.1 = (bf16[64,4096]{1,0:T(8,128)(2,1)S(1)}, bf16[64,4096]{1,0:T(8,128)(2,1)S(1)}, u32[]{:S(2)}, u32[]{:S(2)}) collective-permute-start(bf16[64,4096]{1,0:T(8,128)(2,1)S(1)} %fusion.27), channel_id=1, source_target_pairs={{0,2},{1,3},{2,0},{3,1},{4,6},{5,7},{6,4},{7,5},{8,10},{9,11},{10,... | collective-permute-start | bytes 1572872 | tf_op jit(solution)/shard_map/ppermute | solution.py:152
  178.9 12.0 %collective-permute-done.1 = bf16[64,4096]{1,0:T(8,128)(2,1)S(1)} collective-permute-done((bf16[64,4096]{1,0:T(8,128)(2,1)S(1)}, bf16[64,4096]{1,0:T(8,128)(2,1)S(1)}, u32[]{:S(2)}, u32[]{:S(2)}) %collective-permute-start.1) | collective-permute-done | bytes 524320 | tf_op jit(solution)/shard_map/ppermute | solution.py:152
  190.9 0.9 fusion.16
  (33 shorter events, 2.1 us)
Async XLA Ops:
  0.0 156.5 %copy-start = (bf16[256,256]{1,0:T(8,128)(2,1)S(1)}, bf16[256,256]{1,0:T(8,128)(2,1)}, u32[]{:S(2)}) copy-start(bf16[256,256]{1,0:T(8,128)(2,1)} %param.11) | copy-start | bytes 393220
  4.8 26.4 %all-to-all-start = ((bf16[32,128,128]{2,1,0:T(8,128)(2,1)}), bf16[32,128,128]{2,1,0:T(8,128)(2,1)S(1)}, u32[]{:S(2)}, u32[]{:S(2)}) async-start(bf16[32,128,128]{2,1,0:T(8,128)(2,1)} %copy.94), calls=%async_computation | async-start | bytes 2097152 | tf_op jit(solution)/shard_map/all_to_all | solution.py:53
  39.5 31.7 %all-to-all-start.1 = ((bf16[32,2,2,64,128]{4,3,1,2,0:T(8,128)(2,1)}), bf16[32,2,2,64,128]{4,3,1,2,0:T(8,128)(2,1)S(1)}, u32[]{:S(2)}, u32[]{:S(2)}) async-start(bf16[32,2,2,64,128]{4,3,1,2,0:T(8,128)(2,1)} %pad_maximum_fusion.2), calls=%async_computation.1 | async-start | bytes 4194304 | tf_op jit(solution)/shard_map/all_to_all | solution.py:69
  118.2 2.9 %copy-start.1 = (f32[32,2,64,128]{3,2,1,0:T(8,128)S(1)}, f32[32,2,64,128]{3,2,1,0:T(8,128)}, u32[]{:S(2)}) copy-start(f32[32,2,64,128]{3,2,1,0:T(8,128)} %get-tuple-element.20) | copy-start | bytes 6291460
  151.4 15.0 %copy-start.2 = (bf16[64,4096]{1,0:T(8,128)(2,1)S(1)}, bf16[64,4096]{1,0:T(8,128)(2,1)}, u32[]{:S(2)}) copy-start(bf16[64,4096]{1,0:T(8,128)(2,1)} %param.7) | copy-start | bytes 1572868
  152.5 13.9 %all-to-all-start.3 = ((bf16[32,64,128]{2,1,0:T(8,128)(2,1)}), bf16[32,64,128]{2,1,0:T(8,128)(2,1)S(1)}, u32[]{:S(2)}, u32[]{:S(2)}) async-start(bf16[32,64,128]{2,1,0:T(8,128)(2,1)} %copy.113), calls=%async_computation.3 | async-start | bytes 1048576 | tf_op jit(solution)/shard_map/all_to_all | solution.py:133
  166.8 7.6 %collective-permute-start = (bf16[2,64,4096]{2,1,0:T(8,128)(2,1)S(1)}, bf16[2,64,4096]{2,1,0:T(8,128)(2,1)}, u32[]{:S(2)}, u32[]{:S(2)}) collective-permute-start(bf16[2,64,4096]{2,1,0:T(8,128)(2,1)S(1)} %convolution_convert_fusion), channel_id=1, source_target_pairs={{0,1},{1,0},{2,3},{3,2},{4,5},{5,4},{6,7},{7,6},{8,9},{9,8},{10,11... | collective-permute-start | bytes 3145736 | tf_op jit(solution)/shard_map/ppermute | solution.py:148
  176.2 14.7 %collective-permute-start.1 = (bf16[64,4096]{1,0:T(8,128)(2,1)S(1)}, bf16[64,4096]{1,0:T(8,128)(2,1)S(1)}, u32[]{:S(2)}, u32[]{:S(2)}) collective-permute-start(bf16[64,4096]{1,0:T(8,128)(2,1)S(1)} %fusion.27), channel_id=1, source_target_pairs={{0,2},{1,3},{2,0},{3,1},{4,6},{5,7},{6,4},{7,5},{8,10},{9,11},{10,... | collective-permute-start | bytes 1572872 | tf_op jit(solution)/shard_map/ppermute | solution.py:152
where the time goes:
time: 194 us; the launch traced here: 192 us
  waiting for transfers between devices  67.4 us (35%)
  matrix products  43.3 us (22%)
  starting transfers between devices  25.9 us (13%)
  local copies, waits for them, and re-layouts  19.7 us (10%)
  blocking collectives  17.7 us (9%)
  other arithmetic  17.2 us (9%)
    all_to_all x1, waiting for transfers between devices, body(): recv = lax.all_to_all(spread, 'seq', 0, 0, tiled=True).astype(f32)  27.1 us
    dot_general x8, matrix products, minor(): return jnp.einsum('...b,bm->...m', data, table, precision=HIGH)  25.2 us
    all_to_all x1, blocking collectives, body(): moved = lax.all_to_all(reverted, 'seq', 0, 0, tiled=True).astype(f32)  17.7 us
    all_to_all x1, waiting for transfers between devices, body(): got = lax.all_to_all(send, 'seq', 0, 0, tiled=True).astype(f32)  16.2 us
    dot_general x16, matrix products, major(): return jnp.einsum('qk,k...->q...', table, data, precision=HIGH)  16 us
    ppermute x1, waiting for transfers between devices, body(): lax.ppermute(send_chip.astype(bf16), 'tp', cross).astype(f32)  12 us
    all_to_all x1, waiting for transfers between devices, body(): arrived = lax.all_to_all(merged.astype(bf16), 'seq', 0, 0, tiled=True)  9.74 us
    all_to_all x1, starting transfers between devices, body(): got = lax.all_to_all(send, 'seq', 0, 0, tiled=True).astype(f32)  9.71 us
  transfers between devices with their start and end apart: 5, of which 5 were waited for; matrix products, arithmetic and copies ran while one was open for 0% of the time, Pallas kernels for 0%

commit v1 on v0

--- a/solution.py
+++ b/solution.py
@@ -29,11 +29,6 @@
 
 def minor(data, table):
     return jnp.einsum("...b,bm->...m", data, table, precision=HIGH)
-
-
-def negated_grid(flipped):
-    tail = jnp.roll(flipped[-1:], 1, axis=flipped.ndim - 1)
-    return jnp.concatenate([tail, flipped[:-1]], axis=0)
 
 
 def body(query_gate, key_gate, value_input, long_filter, out_weight):
@@ -81,8 +76,13 @@
     spec_imag = minor(twist_imag, cos_i) - minor(twist_real, sin_i)
 
     def self_paired(parts):
-        flipped = [jnp.flip(part, axis=(0, 3)) for part in parts]
-        return tuple(jnp.stack([negated_grid(f[:, 0]), f[:, 1]], axis=1) for f in flipped)
+        slot = lax.broadcasted_iota(jnp.int32, parts[0].shape, 1)
+        out = []
+        for part in parts:
+            shifted = jnp.where(slot == 0, jnp.roll(part, -1, axis=0), part)
+            flipped = jnp.flip(shifted, axis=(0, 3))
+            out.append(flipped.at[0, 0].set(jnp.roll(flipped[0, 0], 1, axis=-1)))
+        return tuple(out)
 
     def cross_paired(parts):
         return tuple(jnp.flip(part, axis=(0, 1, 3)) for part in parts)

time: 194 us -> 191 us (0.985)
  other arithmetic: 17.2 us -> 13.3 us
    rev x0 -> x2, local copies, waits for them, and re-layouts: none -> 8.51 us  [self_paired(): flipped = jnp.flip(shifted, axis=(0, 3))]
    slice x14 -> x10, local copies, waits for them, and re-layouts: 11 us -> 2.92 us  [the longest x4 1.84 us: self_paired(): shifted = jnp.where(slot == 0, jnp.roll(part, -1, axis=0), part)]
    another operation x3 -> x0, other arithmetic: 6.92 us -> none  [self_paired(): jnp.stack([negated_grid(f[:, 0]), f[:, 1]], axis=1)]
    cond x0 -> x4, local copies, waits for them, and re-layouts: none -> 2.84 us
    select_n x0 -> x1, other arithmetic: none -> 2.26 us  [self_paired(): shifted = jnp.where(slot == 0, jnp.roll(part, -1, axis=0), part)]
    another operation x2 -> x0, local copies, waits for them, and re-layouts: 1.98 us -> none
where the time goes in v1:
time: 191 us; the launch traced here: 189 us
  waiting for transfers between devices  67.4 us (35%)
  matrix products  43.2 us (23%)
  starting transfers between devices  25.9 us (14%)
  local copies, waits for them, and re-layouts  21 us (11%)
  blocking collectives  17.7 us (9%)
  other arithmetic  13.3 us (7%)
    all_to_all x1, waiting for transfers between devices, body(): recv = lax.all_to_all(spread, 'seq', 0, 0, tiled=True).astype(f32)  27.1 us
    dot_general x8, matrix products, minor(): return jnp.einsum('...b,bm->...m', data, table, precision=HIGH)  25.1 us
    all_to_all x1, blocking collectives, body(): moved = lax.all_to_all(reverted, 'seq', 0, 0, tiled=True).astype(f32)  17.7 us
    all_to_all x1, waiting for transfers between devices, body(): got = lax.all_to_all(send, 'seq', 0, 0, tiled=True).astype(f32)  16.2 us
    dot_general x16, matrix products, major(): return jnp.einsum('qk,k...->q...', table, data, precision=HIGH)  16 us
    ppermute x1, waiting for transfers between devices, body(): lax.ppermute(send_chip.astype(bf16), 'tp', cross).astype(f32)  12 us
    all_to_all x1, waiting for transfers between devices, body(): arrived = lax.all_to_all(merged.astype(bf16), 'seq', 0, 0, tiled=True)  9.74 us
    all_to_all x1, starting transfers between devices, body(): got = lax.all_to_all(send, 'seq', 0, 0, tiled=True).astype(f32)  9.71 us
  transfers between devices with their start and end apart: 5, of which 5 were waited for; matrix products, arithmetic and copies ran while one was open for 0% of the time, Pallas kernels for 0%

profile of v1, /device:TPU:1, one launch (start us, length us, event | category | flops | bytes accessed | tf_op | source)
XLA Modules:
  0.0 189.2 jit_solution(7913259149930414523)
XLA Ops:
  0.0 1.3 convert_element_type.149
  1.3 1.3 multiply_convert_fusion
  2.8 0.7 copy.83
  3.5 1.3 copy.84
  4.8 9.7 %all-to-all-start = ((bf16[32,128,128]{2,1,0:T(8,128)(2,1)}), bf16[32,128,128]{2,1,0:T(8,128)(2,1)S(1)}, u32[]{:S(2)}, u32[]{:S(2)}) async-start(bf16[32,128,128]{2,1,0:T(8,128)(2,1)} %copy.84), calls=%async_computation | async-start | bytes 2097152 | tf_op jit(solution)/shard_map/all_to_all | solution.py:48
  14.8 0.2 fusion.111
  15.0 16.2 %all-to-all-done = bf16[32,128,128]{2,1,0:T(8,128)(2,1)S(1)} async-done(((bf16[32,128,128]{2,1,0:T(8,128)(2,1)}), bf16[32,128,128]{2,1,0:T(8,128)(2,1)S(1)}, u32[]{:S(2)}, u32[]{:S(2)}) %all-to-all-start) | async-done | bytes 1048608 | tf_op jit(solution)/shard_map/all_to_all | solution.py:48
  31.3 0.9 fusion.37
  32.2 0.9 fusion.33
  33.0 1.0 convolution_add_fusion.1
  34.1 1.5 add_convert_fusion
  35.6 1.2 copy.87
  36.8 1.2 copy.88
  38.0 1.5 pad_maximum_fusion
  39.5 4.3 %all-to-all-start.1 = ((bf16[32,2,2,64,128]{4,3,1,2,0:T(8,128)(2,1)}), bf16[32,2,2,64,128]{4,3,1,2,0:T(8,128)(2,1)S(1)}, u32[]{:S(2)}, u32[]{:S(2)}) async-start(bf16[32,2,2,64,128]{4,3,1,2,0:T(8,128)(2,1)} %pad_maximum_fusion), calls=%async_computation.1 | async-start | bytes 4194304 | tf_op jit(solution)/shard_map/all_to_all | solution.py:64
  43.9 0.2 fusion.107
  44.2 27.1 %all-to-all-done.1 = bf16[32,2,2,64,128]{4,3,1,2,0:T(8,128)(2,1)S(1)} async-done(((bf16[32,2,2,64,128]{4,3,1,2,0:T(8,128)(2,1)}), bf16[32,2,2,64,128]{4,3,1,2,0:T(8,128)(2,1)S(1)}, u32[]{:S(2)}, u32[]{:S(2)}) %all-to-all-start.1) | async-done | bytes 2097184 | tf_op jit(solution)/shard_map/all_to_all | solution.py:64
  71.2 0.2 fusion.247
  71.4 1.1 fusion.25
  72.5 1.1 fusion.26
  73.7 1.1 convolution_add_fusion
  74.8 1.6 multiply_add_fusion
  76.5 2.2 %fusion.4 = f32[32,2,64,128]{3,2,1,0:T(8,128)S(1)} fusion(f32[32,2,64,128]{3,0,2,1:T(8,128)S(1)} %get-tuple-element.54), kind=kOutput, calls=%fused_computation.20 | convolution fusion | flops 402882560 | bytes 4194304 | tf_op jit(solution)/shard_map/...b,bm->...m/dot_general | solution.py:31
  78.7 2.3 %fusion.2 = f32[32,2,64,128]{3,2,1,0:T(8,128)S(1)} fusion(f32[32,2,64,128]{3,0,2,1:T(8,128)S(1)} %get-tuple-element.54), kind=kOutput, calls=%fused_computation.18 | convolution fusion | flops 402882560 | bytes 4194304 | tf_op jit(solution)/shard_map/...b,bm->...m/dot_general | solution.py:31
  81.0 14.9 %fusion.10 = f32[32,2,64,128]{3,2,1,0:T(8,128)} fusion(f32[32,2,64,128]{3,2,1,0:T(8,128)S(1)} %fusion.4, f32[32,2,64,128]{3,0,2,1:T(8,128)S(1)} %get-tuple-element.53), kind=kOutput, calls=%fused_computation.28 | convolution fusion | flops 403406848 | bytes 6291456 | tf_op jit(solution)/shard_map/...b,bm->...m/dot_general | solution.py:31
  95.9 2.3 %fusion.13 = f32[32,2,64,128]{3,2,1,0:T(8,128)S(1)} fusion(f32[32,2,64,128]{3,2,1,0:T(8,128)S(1)} %fusion.2, f32[32,2,64,128]{3,0,2,1:T(8,128)S(1)} %get-tuple-element.53), kind=kOutput, calls=%fused_computation.29 | convolution fusion | flops 403406848 | bytes 6291456 | tf_op jit(solution)/shard_map/...b,bm->...m/dot_general | solution.py:31
  98.2 17.3 %conditional.1 = ((f32[32,2,64,128]{3,2,1,0:T(8,128)}, f32[32,2,64,128]{3,2,1,0:T(8,128)})) conditional(s32[]{:T(128)} %convert_element_type.153, (f32[32,2,64,128]{3,2,1,0:T(8,128)}, f32[32,2,64,128]{3,2,1,0:T(8,128)S(1)}) %tuple.21, (f32[32,2,64,128]{3,2,1,0:T(8,128)}, f32[32,2,64,128]{3,2,1,0:T(8,128)S(1)}) %tuple.21), branch_computations={%region_0.1_spmd, %region_1.2_spmd} | conditional | flops 2113538 | bytes 46531652 | solution.py:90
  98.2 1.7 slice.122
  99.9 0.1 slice.128
  100.1 1.4 copy-done.1
  101.6 2.3 %maximum_select_fusion.1 = (f32[32,2,64,128]{3,2,1,0:T(8,128)}, f32[32,2,64,128]{3,2,1,0:T(8,128)S(1)}) fusion(f32[32,2,64,128]{3,2,1,0:T(8,128)S(1)} %get-tuple-element.40, f32[1,2,64,128]{3,2,1,0:T(8,128)S(1)} %slice.129, f32[31,2,64,128]{3,2,1,0:T(8,128)S(1)} %slice.128, pred[2]{0:T(512)(128)(4,1)S(1)} %iota_compare_fusion, ...), kind=kLoop, calls=%fused_computation.1 | loop fusion | flops 2097152 | bytes 12582914 | tf_op jit(solution)/shard_map/cond/branch_1_fun/jit(_where)/select_n | solution.py:82
  103.8 1.4 copy-done.2
  105.4 0.8 slice.173
  106.3 4.3 %rev.12 = f32[32,2,64,128]{3,2,1,0:T(8,128)} reverse(f32[32,2,64,128]{3,2,1,0:T(8,128)} %copy-done.2), dimensions={0,3} | reverse | bytes 4194304 | tf_op jit(solution)/shard_map/cond/branch_1_fun/jit(_flip)/rev | solution.py:83
  110.6 4.2 %rev.13 = f32[32,2,64,128]{3,2,1,0:T(8,128)} reverse(f32[32,2,64,128]{3,2,1,0:T(8,128)} %get-tuple-element.45), dimensions={0,3} | reverse | bytes 4194304 | tf_op jit(solution)/shard_map/cond/branch_1_fun/jit(_flip)/rev | solution.py:83
  114.8 0.7 fusion
  115.5 2.9 %add_multiply_fusion.1 = (f32[32,2,64,128]{3,2,1,0:T(8,128)S(1)}, f32[32,2,64,128]{3,2,1,0:T(8,128)S(1)}) fusion(f32[32,2,64,128]{3,2,1,0:T(8,128)} %fusion.10, f32[32,2,64,128]{3,2,1,0:T(8,128)} %get-tuple-element.43), kind=kLoop, calls=%fused_computation.13 | loop fusion | flops 2097152 | bytes 8388608 | tf_op jit(solution)/shard_map/mul | solution.py:94
  118.4 0.5 subtract_multiply_fusion.1
  118.9 1.0 add_subtract_fusion
  119.9 0.8 fusion.46
  120.8 0.8 fusion.48
  121.6 0.8 convolution_add_fusion.3
  122.4 0.9 multiply_add_fusion.1
  123.4 1.2 fusion.19
  124.6 1.2 fusion.23
  125.7 1.2 convolution_add_fusion.2
  126.9 1.5 fusion.27
  128.5 0.4 copy.99
  128.9 17.7 %all_to_all.20 = bf16[32,2,2,32,128]{4,3,1,2,0:T(8,128)(2,1)S(1)} all-to-all(bf16[32,2,2,32,128]{4,3,1,2,0:T(8,128)(2,1)S(1)} %copy.99), channel_id=1, replica_groups=mesh['seq'=32,'tp'=4] {'seq'}, dimensions={0} | all-to-all | bytes 2097152 | tf_op jit(solution)/shard_map/all_to_all | solution.py:125
  146.7 0.1 copy.100
  146.9 0.4 fusion.31
  147.3 0.4 fusion.32
  147.7 0.5 convolution_subtract_fusion.4
  148.2 0.5 convolution_add_fusion.4
  148.8 1.0 copy.103
  149.8 4.0 %all-to-all-start.3 = ((bf16[32,64,128]{2,1,0:T(8,128)(2,1)}), bf16[32,64,128]{2,1,0:T(8,128)(2,1)S(1)}, u32[]{:S(2)}, u32[]{:S(2)}) async-start(bf16[32,64,128]{2,1,0:T(8,128)(2,1)} %copy.103), calls=%async_computation.3 | async-start | bytes 1048576 | tf_op jit(solution)/shard_map/all_to_all | solution.py:133
  153.9 9.7 %all-to-all-done.3 = bf16[32,64,128]{2,1,0:T(8,128)(2,1)S(1)} async-done(((bf16[32,64,128]{2,1,0:T(8,128)(2,1)}), bf16[32,64,128]{2,1,0:T(8,128)(2,1)S(1)}, u32[]{:S(2)}, u32[]{:S(2)}) %all-to-all-start.3) | async-done | bytes 524320 | tf_op jit(solution)/shard_map/all_to_all | solution.py:133
  163.7 0.4 convolution_convert_fusion
  164.1 5.2 %collective-permute-start = (bf16[2,64,4096]{2,1,0:T(8,128)(2,1)S(1)}, bf16[2,64,4096]{2,1,0:T(8,128)(2,1)}, u32[]{:S(2)}, u32[]{:S(2)}) collective-permute-start(bf16[2,64,4096]{2,1,0:T(8,128)(2,1)S(1)} %convolution_convert_fusion), channel_id=1, source_target_pairs={{0,1},{1,0},{2,3},{3,2},{4,5},{5,4},{6,7},{7,6},{8,9},{9,8},{10,11... | collective-permute-start | bytes 3145736 | tf_op jit(solution)/shard_map/ppermute | solution.py:148
  169.3 2.4 %collective-permute-done = bf16[2,64,4096]{2,1,0:T(8,128)(2,1)} collective-permute-done((bf16[2,64,4096]{2,1,0:T(8,128)(2,1)S(1)}, bf16[2,64,4096]{2,1,0:T(8,128)(2,1)}, u32[]{:S(2)}, u32[]{:S(2)}) %collective-permute-start) | collective-permute-done | bytes 1048608 | tf_op jit(solution)/shard_map/ppermute | solution.py:148
  171.7 1.6 convert_add_fusion
  173.4 2.7 %collective-permute-start.1 = (bf16[64,4096]{1,0:T(8,128)(2,1)S(1)}, bf16[64,4096]{1,0:T(8,128)(2,1)S(1)}, u32[]{:S(2)}, u32[]{:S(2)}) collective-permute-start(bf16[64,4096]{1,0:T(8,128)(2,1)S(1)} %fusion.29), channel_id=1, source_target_pairs={{0,2},{1,3},{2,0},{3,1},{4,6},{5,7},{6,4},{7,5},{8,10},{9,11},{10,... | collective-permute-start | bytes 1572872 | tf_op jit(solution)/shard_map/ppermute | solution.py:152
  176.2 12.0 %collective-permute-done.1 = bf16[64,4096]{1,0:T(8,128)(2,1)S(1)} collective-permute-done((bf16[64,4096]{1,0:T(8,128)(2,1)S(1)}, bf16[64,4096]{1,0:T(8,128)(2,1)S(1)}, u32[]{:S(2)}, u32[]{:S(2)}) %collective-permute-start.1) | collective-permute-done | bytes 524320 | tf_op jit(solution)/shard_map/ppermute | solution.py:152
  188.1 0.9 fusion.18
  (33 shorter events, 1.3 us)
Async XLA Ops:
  0.0 153.8 %copy-start = (bf16[256,256]{1,0:T(8,128)(2,1)S(1)}, bf16[256,256]{1,0:T(8,128)(2,1)}, u32[]{:S(2)}) copy-start(bf16[256,256]{1,0:T(8,128)(2,1)} %param.15) | copy-start | bytes 393220
  4.8 26.4 %all-to-all-start = ((bf16[32,128,128]{2,1,0:T(8,128)(2,1)}), bf16[32,128,128]{2,1,0:T(8,128)(2,1)S(1)}, u32[]{:S(2)}, u32[]{:S(2)}) async-start(bf16[32,128,128]{2,1,0:T(8,128)(2,1)} %copy.84), calls=%async_computation | async-start | bytes 2097152 | tf_op jit(solution)/shard_map/all_to_all | solution.py:48
  39.5 31.7 %all-to-all-start.1 = ((bf16[32,2,2,64,128]{4,3,1,2,0:T(8,128)(2,1)}), bf16[32,2,2,64,128]{4,3,1,2,0:T(8,128)(2,1)S(1)}, u32[]{:S(2)}, u32[]{:S(2)}) async-start(bf16[32,2,2,64,128]{4,3,1,2,0:T(8,128)(2,1)} %pad_maximum_fusion), calls=%async_computation.1 | async-start | bytes 4194304 | tf_op jit(solution)/shard_map/all_to_all | solution.py:64
  99.9 1.6 copy-start.1
  103.8 1.4 copy-start.2
  115.5 2.9 %copy-start.3 = (f32[32,2,64,128]{3,2,1,0:T(8,128)S(1)}, f32[32,2,64,128]{3,2,1,0:T(8,128)}, u32[]{:S(2)}) copy-start(f32[32,2,64,128]{3,2,1,0:T(8,128)} %get-tuple-element.44) | copy-start | bytes 6291460
  148.6 15.0 %copy-start.4 = (bf16[64,4096]{1,0:T(8,128)(2,1)S(1)}, bf16[64,4096]{1,0:T(8,128)(2,1)}, u32[]{:S(2)}) copy-start(bf16[64,4096]{1,0:T(8,128)(2,1)} %param.11) | copy-start | bytes 1572868
  149.8 13.9 %all-to-all-start.3 = ((bf16[32,64,128]{2,1,0:T(8,128)(2,1)}), bf16[32,64,128]{2,1,0:T(8,128)(2,1)S(1)}, u32[]{:S(2)}, u32[]{:S(2)}) async-start(bf16[32,64,128]{2,1,0:T(8,128)(2,1)} %copy.103), calls=%async_computation.3 | async-start | bytes 1048576 | tf_op jit(solution)/shard_map/all_to_all | solution.py:133
  164.1 7.6 %collective-permute-start = (bf16[2,64,4096]{2,1,0:T(8,128)(2,1)S(1)}, bf16[2,64,4096]{2,1,0:T(8,128)(2,1)}, u32[]{:S(2)}, u32[]{:S(2)}) collective-permute-start(bf16[2,64,4096]{2,1,0:T(8,128)(2,1)S(1)} %convolution_convert_fusion), channel_id=1, source_target_pairs={{0,1},{1,0},{2,3},{3,2},{4,5},{5,4},{6,7},{7,6},{8,9},{9,8},{10,11... | collective-permute-start | bytes 3145736 | tf_op jit(solution)/shard_map/ppermute | solution.py:148
  173.4 14.7 %collective-permute-start.1 = (bf16[64,4096]{1,0:T(8,128)(2,1)S(1)}, bf16[64,4096]{1,0:T(8,128)(2,1)S(1)}, u32[]{:S(2)}, u32[]{:S(2)}) collective-permute-start(bf16[64,4096]{1,0:T(8,128)(2,1)S(1)} %fusion.29), channel_id=1, source_target_pairs={{0,2},{1,3},{2,0},{3,1},{4,6},{5,7},{6,4},{7,5},{8,10},{9,11},{10,... | collective-permute-start | bytes 1572872 | tf_op jit(solution)/shard_map/ppermute | solution.py:152
